TPU v7x, 512 devices: a whole 4x8x8 slice. The times are simulated.
512 devices in a mesh: ctx: 64 (over z_lo, y, core), ch: 8 (over z_hi, x).
Axes of the slice: x: 4, y: 8, z: 8 (z_hi: 2, z_lo: 4; z = z_hi * 4 + z_lo), core: 2. Of those that a mesh axis runs over, the one named last changes fastest.
Arguments:
- query_in: bfloat16 [16384, 4096], P('ctx', 'ch'), may hold values from -6 to 6
- key_in: bfloat16 [16384, 4096], P('ctx', 'ch'), may hold values from -6 to 6
- value_in: bfloat16 [16384, 4096], P('ctx', 'ch'), may hold values from -6 to 6
- short_weight: float32 [3, 3, 4096], P(None, None, 'ch'), may hold values from -3 to 3
- long_filter: bfloat16 [32, 768], P('ch'), may hold values from -1.1 to 1.1
- skip_weight: float32 [4096], P('ch'), may hold values from -1 to 1
- out_weight: bfloat16 [4096, 4096], P('ctx', 'ch'), may hold values from -0.09375 to 0.09375
- doc_ids: int32 [16384], P('ctx'), may hold values from 0 to 41, as said below
- out_grad: bfloat16 [16384, 4096], P('ctx', 'ch'), may hold values from -6 to 6
Outputs:
- layer_out: bfloat16 [16384, 4096], P('ctx', 'ch')
- grad_query: bfloat16 [16384, 4096], P('ctx', 'ch')
- grad_key: bfloat16 [16384, 4096], P('ctx', 'ch')
- grad_value: bfloat16 [16384, 4096], P('ctx', 'ch')
Inputs may be any that keep to these rules, and one draw needn't show every extreme that they name: doc_ids never falls along the tokens; every number from 0 to 41 occurs; every document has at most 768 tokens and one has exactly 768.
All inputs are finite; a program needn't handle non-finite values.
Results may differ from a plain program's by a relative error of at most 0.0058.
Values may be sent and summed in bfloat16 or wider, within the bound.
No kernel may reach another device: no remote copies, remote signals or barrier semaphores. Data moves between devices by JAX's collectives and lax.ppermute only.
A program may use at most 64 MiB of HBM per device.

v0:
```python
import jax
import jax.numpy as jnp
from jax import lax
from jax.sharding import PartitionSpec as P

HOPS = 3


def shifted(array, axis, by):
    size = lax.axis_size(axis)
    pairs = [(i, i + by) for i in range(size) if 0 <= i + by < size]
    return lax.ppermute(array, axis, pairs)


def toeplitz_tiles(long_filter, row_count, hop_count):
    group_count, span_len = long_filter.shape
    padded = jnp.concatenate(
        [
            jnp.zeros((group_count, row_count), long_filter.dtype),
            long_filter,
            jnp.zeros((group_count, (hop_count + 3) * row_count - span_len), long_filter.dtype),
        ],
        axis=1,
    )
    tiles_list = []
    for distance in range(hop_count + 1):
        window = padded[:, distance * row_count + 1 : distance * row_count + 1 + 2 * row_count]
        cyclic = jnp.concatenate(
            [
                window[:, row_count - 1 : 2 * row_count - 1],
                jnp.zeros((group_count, 1), window.dtype),
                window[:, : row_count - 1],
            ],
            axis=1,
        )
        repeated = jnp.tile(cyclic, (1, row_count))[:, : row_count * (2 * row_count - 1)]
        tiles_list.append(
            repeated.reshape(group_count, row_count, 2 * row_count - 1)[:, :, :row_count]
        )
    return tiles_list


def apply_forward(band_tile, source):
    row_count, channels = source.shape
    grouped = source.reshape(row_count, band_tile.shape[0], -1)
    return jnp.einsum(
        "gst,sgc->tgc", band_tile, grouped, preferred_element_type=jnp.float32
    ).reshape(row_count, channels)


def apply_adjoint(band_tile, source):
    row_count, channels = source.shape
    grouped = source.reshape(row_count, band_tile.shape[0], -1)
    return jnp.einsum(
        "gst,tgc->sgc", band_tile, grouped, preferred_element_type=jnp.float32
    ).reshape(row_count, channels)


def causal_taps(extended, weights, ext_ids, doc_ids):
    row_count = doc_ids.shape[0]
    summed = jnp.zeros((row_count, extended.shape[1]), jnp.float32)
    for offset in range(3):
        first_row = 2 - offset
        same_doc = ext_ids[first_row : first_row + row_count] == doc_ids
        summed = summed + jnp.where(
            same_doc[:, None],
            weights[offset][None, :]
            * extended[first_row : first_row + row_count].astype(jnp.float32),
            0.0,
        )
    return summed


def anti_taps(extended, weights, ext_ids, doc_ids):
    row_count = doc_ids.shape[0]
    summed = jnp.zeros((row_count, extended.shape[1]), jnp.float32)
    for offset in range(3):
        same_doc = ext_ids[offset : offset + row_count] == doc_ids
        summed = summed + jnp.where(
            same_doc[:, None],
            weights[offset][None, :] * extended[offset : offset + row_count].astype(jnp.float32),
            0.0,
        )
    return summed


def local(
    query_in,
    key_in,
    value_in,
    short_weight,
    long_filter,
    skip_weight,
    out_weight,
    doc_ids,
    out_grad,
):
    row_count, channels = query_in.shape
    before_ids = shifted(doc_ids[-2:] + 1, "ctx", 1) - 1
    after_ids = shifted(doc_ids[:2] + 1, "ctx", -1) - 1
    first_id = doc_ids[0]
    last_id = doc_ids[-1]
    prev_last = before_ids[1]
    next_first = after_ids[0]
    single_doc = first_id == last_id
    joins_next = next_first == last_id
    joins_prev = prev_last == first_id
    prev_rows = shifted((query_in[-2:], key_in[-2:], value_in[-2:]), "ctx", 1)
    back_ids = jnp.concatenate([before_ids, doc_ids])
    query_short = causal_taps(
        jnp.concatenate([prev_rows[0], query_in]), short_weight[0], back_ids, doc_ids
    )
    key_short = causal_taps(
        jnp.concatenate([prev_rows[1], key_in]), short_weight[1], back_ids, doc_ids
    )
    value_short = causal_taps(
        jnp.concatenate([prev_rows[2], value_in]), short_weight[2], back_ids, doc_ids
    )
    gated = (key_short * value_short).astype(jnp.bfloat16)
    tiles_list = toeplitz_tiles(long_filter, row_count, HOPS)
    same_doc = doc_ids[:, None] == doc_ids[None, :]
    diagonal = jnp.where(same_doc[None], tiles_list[0], jnp.zeros((), tiles_list[0].dtype))
    head_rows = (doc_ids == first_id)[:, None]
    tail_rows = (doc_ids == last_id)[:, None]
    zero_half = jnp.zeros((), gated.dtype)

    def cross_term(is_live, product, band_tile, source):
        summand = jnp.where(is_live, product(band_tile, source), 0.0)
        return summand

    mixed = apply_forward(diagonal, gated) + skip_weight[None, :] * gated.astype(jnp.float32)
    own_tail = jnp.where(tail_rows, gated, zero_half)
    moving = jnp.where(joins_next, own_tail, zero_half)
    for distance in range(1, HOPS + 1):
        moving = shifted(moving, "ctx", 1)
        is_live = jnp.any(moving != 0)
        mixed = mixed + jnp.where(
            head_rows, cross_term(is_live, apply_forward, tiles_list[distance], moving), 0.0
        )
        moving = jnp.where(single_doc & joins_next, moving, zero_half)
    pre_gate = (query_short * mixed).astype(jnp.bfloat16)
    weight_rows = lax.all_gather(out_weight, "ctx", axis=0, tiled=True)
    matched = weight_rows
    out_sum = jnp.dot(
        lax.all_gather(pre_gate, "ch", axis=1, tiled=True),
        matched,
        preferred_element_type=jnp.float32,
    )
    matched = weight_rows
    grad_cols = lax.psum_scatter(
        lax.dot_general(
            matched, out_grad, (((1,), (1,)), ((), ())), preferred_element_type=jnp.float32
        ),
        "ch",
        scatter_dimension=0,
        tiled=True,
    )
    layer_out = out_sum.astype(jnp.bfloat16)
    grad_pre = jnp.transpose(grad_cols)
    grad_query_short = (grad_pre * mixed).astype(jnp.bfloat16)
    grad_mixed = (grad_pre * query_short).astype(jnp.bfloat16)
    own_head = jnp.where(head_rows, grad_mixed, zero_half)
    grad_gated = apply_adjoint(diagonal, grad_mixed) + skip_weight[None, :] * grad_mixed.astype(
        jnp.float32
    )
    moving_back = jnp.where(joins_prev, own_head, zero_half)
    for distance in range(1, HOPS + 1):
        moving_back = shifted(moving_back, "ctx", -1)
        is_live = jnp.any(moving_back != 0)
        grad_gated = grad_gated + jnp.where(
            tail_rows, cross_term(is_live, apply_adjoint, tiles_list[distance], moving_back), 0.0
        )
        moving_back = jnp.where(single_doc & joins_prev, moving_back, zero_half)
    grad_key_short = (grad_gated * value_short).astype(jnp.bfloat16)
    grad_value_short = (grad_gated * key_short).astype(jnp.bfloat16)
    next_rows = shifted((grad_query_short[:2], grad_key_short[:2], grad_value_short[:2]), "ctx", -1)
    ahead_ids = jnp.concatenate([doc_ids, after_ids])
    grad_query = anti_taps(
        jnp.concatenate([grad_query_short, next_rows[0]]), short_weight[0], ahead_ids, doc_ids
    ).astype(jnp.bfloat16)
    grad_key = anti_taps(
        jnp.concatenate([grad_key_short, next_rows[1]]), short_weight[1], ahead_ids, doc_ids
    ).astype(jnp.bfloat16)
    grad_value = anti_taps(
        jnp.concatenate([grad_value_short, next_rows[2]]), short_weight[2], ahead_ids, doc_ids
    ).astype(jnp.bfloat16)
    return (layer_out, grad_query, grad_key, grad_value)


def solution(mesh):
    return jax.shard_map(
        local,
        mesh=mesh,
        in_specs=(
            P("ctx", "ch"),
            P("ctx", "ch"),
            P("ctx", "ch"),
            P(None, None, "ch"),
            P("ch", None),
            P("ch"),
            P("ctx", "ch"),
            P("ctx"),
            P("ctx", "ch"),
        ),
        out_specs=(P("ctx", "ch"), P("ctx", "ch"), P("ctx", "ch"), P("ctx", "ch")),
        check_vma=False,
    )
```

profile of v0, /device:TPU:8, one launch (start us, length us, event | category | flops | bytes accessed | tf_op | source)
XLA Modules:
  0.0 379.9 jit_solution(4327605552182288887)
XLA Ops:
  8.0 125.7 %all-gather.5.cloned.1.call-done = bf16[4096,512]{1,0:T(8,128)(2,1)} async-done(((bf16[64,512]{1,0:T(8,128)(2,1)}), bf16[4096,512]{1,0:T(8,128)(2,1)}) %all-gather.5.cloned.1.call-update) | async-done | bytes 4194320 | tf_op jit(solution)/shard_map/all_gather | solution.py:142
  133.6 5.5 %fusion.39 = f32[4096,256]{1,0:T(8,128)} fusion(bf16[4096,512]{1,0:T(8,128)(2,1)} %all-gather.5.cloned.1.call-done, bf16[256,512]{1,0:T(8,128)(2,1)S(1)} %copy-done), kind=kOutput, calls=%fused_computation.116 | convolution fusion | flops 1073741824 | bytes 8650752 | tf_op jit(solution)/shard_map/dot_general | solution.py:151
  140.4 3.6 collective-permute-start.4
  153.3 2.7 collective-permute-start.3
  165.0 3.3 select_select_fusion.1
  174.5 3.0 reshape.150
  179.7 3.1 reshape.148
  185.0 3.0 reshape.146
  191.4 4.0 %reshape.143 = bf16[4,256,511]{2,1,0:T(8,128)(2,1)} reshape(bf16[4,130816]{1,0:T(4,128)(2,1)} %slice.278) | data formatting | bytes 2093056 | tf_op jit(solution)/shard_map/reshape | solution.py:38
  198.6 3.6 collective-permute-start.6
  203.8 2.6 broadcast_select_fusion.5
  211.0 3.1 collective-permute-done.7
  216.6 59.5 %reduce-scatter.2.cloned.1.call-done = f32[512,256]{1,0:T(8,128)} async-done(((f32[4096,256]{1,0:T(8,128)}), f32[512,256]{1,0:T(8,128)}) %reduce-scatter.2.cloned.1.call-update) | async-done | bytes 524304 | tf_op jit(solution)/shard_map/reduce_scatter | solution.py:150
  276.1 2.9 fusion.6
  285.0 3.4 add_convert_fusion.2
  291.0 2.8 select_select_fusion
  293.7 3.8 collective-permute-start.9
  299.0 2.7 collective-permute-done.9
  302.7 4.1 %collective-permute-start.10 = (bf16[256,512]{0,1:T(8,128)(2,1)S(1)}, bf16[256,512]{0,1:T(8,128)(2,1)S(1)}, u32[]{:S(2)}, u32[]{:S(2)}) collective-permute-start(bf16[256,512]{0,1:T(8,128)(2,1)S(1)} %broadcast_select_fusion.7), channel_id=1, source_target_pairs={{8,0},{16,8},{24,16},{32,24},{40,32},{48,40},{56,48},{64,56},{72,6... | collective-permute-start | bytes 786440 | tf_op jit(solution)/shard_map/ppermute | solution.py:12
  310.7 4.2 %collective-permute-start.11 = (bf16[256,512]{0,1:T(8,128)(2,1)S(1)}, bf16[256,512]{0,1:T(8,128)(2,1)S(1)}, u32[]{:S(2)}, u32[]{:S(2)}) collective-permute-start(bf16[256,512]{0,1:T(8,128)(2,1)S(1)} %broadcast_select_fusion.6), channel_id=1, source_target_pairs={{8,0},{16,8},{24,16},{32,24},{40,32},{48,40},{56,48},{64,56},{72,6... | collective-permute-start | bytes 786440 | tf_op jit(solution)/shard_map/ppermute | solution.py:12
  322.2 3.8 %collective-permute-start.13 = (bf16[2,512]{0,1:T(8,128)(2,1)S(1)}, bf16[2,512]{0,1:T(8,128)(2,1)S(1)}, u32[]{:S(2)}, u32[]{:S(2)}) collective-permute-start(bf16[2,512]{0,1:T(8,128)(2,1)S(1)} %slice.292), channel_id=1, source_target_pairs={{8,0},{16,8},{24,16},{32,24},{40,32},{48,40},{56,48},{64,56},{72,6... | collective-permute-start | bytes 6152 | tf_op jit(solution)/shard_map/ppermute | solution.py:12
  329.5 3.8 collective-permute-start.12
  337.2 31.4 %all-gather.3.cloned.1.call-done = bf16[256,4096]{0,1:T(8,128)(2,1)} async-done(((bf16[256,512]{0,1:T(8,128)(2,1)}), bf16[256,4096]{0,1:T(8,128)(2,1)}) %all-gather.3.cloned.1.call-update) | async-done | bytes 2097168 | tf_op jit(solution)/shard_map/all_gather | solution.py:145
  368.6 4.8 %convolution_convert_fusion = bf16[256,512]{1,0:T(8,128)(2,1)} fusion(bf16[256,4096]{0,1:T(8,128)(2,1)} %all-gather.3.cloned.1.call-done, bf16[4096,512]{1,0:T(8,128)(2,1)} %all-gather.5.cloned.1.call-done), kind=kOutput, calls=%fused_computation | convolution fusion | flops 1073872896 | bytes 6553600 | tf_op jit(solution)/shard_map/dot_general | solution.py:144
  (132 shorter events, 71.6 us)
Async XLA Ops:
  7.2 126.5 %copy-start = (bf16[256,512]{1,0:T(8,128)(2,1)S(1)}, bf16[256,512]{1,0:T(8,128)(2,1)}, u32[]{:S(2)}) copy-start(bf16[256,512]{1,0:T(8,128)(2,1)} %param.17) | copy-start | bytes 786436
  7.2 126.4 %all-gather.5.cloned.1.call-start = ((), (), s32[]{:S(2)}) async-start(), calls=%async_computation.2 | async-start | bytes 4259840 | tf_op jit(solution)/shard_map/all_gather | solution.py:142
  7.9 268.2 %reduce-scatter.2.cloned.1.call-start = ((), (), s32[]{:S(2)}) async-start(), calls=%async_computation.3 | async-start | bytes 4718592 | tf_op jit(solution)/shard_map/reduce_scatter | solution.py:150
  139.2 229.4 %all-gather.3.cloned.1.call-start = ((), (), s32[]{:S(2)}) async-start(), calls=%async_computation.1 | async-start | bytes 2359296 | tf_op jit(solution)/shard_map/all_gather | solution.py:145
  140.4 20.1 %collective-permute-start.4 = (s32[2]{0:T(128)}, s32[2]{0:T(128)}, u32[]{:S(2)}, u32[]{:S(2)}) collective-permute-start(s32[2]{0:T(128)} %get-tuple-element.55), channel_id=1, source_target_pairs={{8,0},{16,8},{24,16},{32,24},{40,32},{48,40},{56,48},{64,56},{72,6... | collective-permute-start | bytes 32 | tf_op jit(solution)/shard_map/ppermute | solution.py:12
  144.0 17.1 %collective-permute-start = (s32[2]{0:T(128)}, s32[2]{0:T(128)}, u32[]{:S(2)}, u32[]{:S(2)}) collective-permute-start(s32[2]{0:T(128)} %get-tuple-element.54), channel_id=1, source_target_pairs={{0,8},{8,16},{16,24},{24,32},{32,40},{40,48},{48,56},{56,64},{64,7... | collective-permute-start | bytes 32 | tf_op jit(solution)/shard_map/ppermute | solution.py:12
  147.5 136.5 %collective-permute-start.1 = (bf16[2,512]{0,1:T(8,128)(2,1)}, bf16[2,512]{0,1:T(8,128)(2,1)}, u32[]{:S(2)}, u32[]{:S(2)}) collective-permute-start(bf16[2,512]{0,1:T(8,128)(2,1)} %copy.26), channel_id=1, source_target_pairs={{0,8},{8,16},{16,24},{24,32},{32,40},{40,48},{48,56},{56,64},{64,7... | collective-permute-start | bytes 6152 | tf_op jit(solution)/shard_map/ppermute | solution.py:12
  150.5 14.5 %collective-permute-start.2 = (bf16[2,512]{0,1:T(8,128)(2,1)}, bf16[2,512]{0,1:T(8,128)(2,1)}, u32[]{:S(2)}, u32[]{:S(2)}) collective-permute-start(bf16[2,512]{0,1:T(8,128)(2,1)} %copy.29), channel_id=1, source_target_pairs={{0,8},{8,16},{16,24},{24,32},{32,40},{40,48},{48,56},{56,64},{64,7... | collective-permute-start | bytes 6152 | tf_op jit(solution)/shard_map/ppermute | solution.py:12
  153.3 11.7 %collective-permute-start.3 = (bf16[2,512]{0,1:T(8,128)(2,1)}, bf16[2,512]{0,1:T(8,128)(2,1)S(1)}, u32[]{:S(2)}, u32[]{:S(2)}) collective-permute-start(bf16[2,512]{0,1:T(8,128)(2,1)} %copy.32), channel_id=1, source_target_pairs={{0,8},{8,16},{16,24},{24,32},{32,40},{40,48},{48,56},{56,64},{64,7... | collective-permute-start | bytes 6152 | tf_op jit(solution)/shard_map/ppermute | solution.py:12
  168.3 29.3 %collective-permute-start.5 = (bf16[256,512]{0,1:T(8,128)(2,1)}, bf16[256,512]{0,1:T(8,128)(2,1)}, u32[]{:S(2)}, u32[]{:S(2)}) collective-permute-start(bf16[256,512]{0,1:T(8,128)(2,1)} %get-tuple-element.18), channel_id=1, source_target_pairs={{0,8},{8,16},{16,24},{24,32},{32,40},{40,48},{48,56},{56,64},{64,7... | collective-permute-start | bytes 786440 | tf_op jit(solution)/shard_map/ppermute | solution.py:12
  198.6 7.9 %collective-permute-start.6 = (bf16[256,512]{0,1:T(8,128)(2,1)S(1)}, bf16[256,512]{0,1:T(8,128)(2,1)S(1)}, u32[]{:S(2)}, u32[]{:S(2)}) collective-permute-start(bf16[256,512]{0,1:T(8,128)(2,1)S(1)} %broadcast_select_fusion.9), channel_id=1, source_target_pairs={{0,8},{8,16},{16,24},{24,32},{32,40},{40,48},{48,56},{56,64},{64,7... | collective-permute-start | bytes 786440 | tf_op jit(solution)/shard_map/ppermute | solution.py:12
  206.5 78.6 %copy-start.10 = (pred[256]{0:T(512)(128)(4,1)S(1)}, pred[256]{0:T(512)(128)(4,1)}, u32[]{:S(2)}) copy-start(pred[256]{0:T(512)(128)(4,1)} %get-tuple-element.45) | copy-start | bytes 772
  206.5 7.7 %collective-permute-start.7 = (bf16[256,512]{0,1:T(8,128)(2,1)S(1)}, bf16[256,512]{0,1:T(8,128)(2,1)S(1)}, u32[]{:S(2)}, u32[]{:S(2)}) collective-permute-start(bf16[256,512]{0,1:T(8,128)(2,1)S(1)} %broadcast_select_fusion.8), channel_id=1, source_target_pairs={{0,8},{8,16},{16,24},{24,32},{32,40},{40,48},{48,56},{56,64},{64,7... | collective-permute-start | bytes 786440 | tf_op jit(solution)/shard_map/ppermute | solution.py:12
  280.3 4.7 %collective-permute-start.8 = (bf16[2,512]{0,1:T(8,128)(2,1)}, bf16[2,512]{0,1:T(8,128)(2,1)}, u32[]{:S(2)}, u32[]{:S(2)}) collective-permute-start(bf16[2,512]{0,1:T(8,128)(2,1)} %slice.286), channel_id=1, source_target_pairs={{8,0},{16,8},{24,16},{32,24},{40,32},{48,40},{56,48},{64,56},{72,6... | collective-permute-start | bytes 6152 | tf_op jit(solution)/shard_map/ppermute | solution.py:12
  293.7 8.0 %collective-permute-start.9 = (bf16[256,512]{0,1:T(8,128)(2,1)}, bf16[256,512]{0,1:T(8,128)(2,1)}, u32[]{:S(2)}, u32[]{:S(2)}) collective-permute-start(bf16[256,512]{0,1:T(8,128)(2,1)} %get-tuple-element.14), channel_id=1, source_target_pairs={{8,0},{16,8},{24,16},{32,24},{40,32},{48,40},{56,48},{64,56},{72,6... | collective-permute-start | bytes 786440 | tf_op jit(solution)/shard_map/ppermute | solution.py:12
  297.5 22.9 %copy-start.2 = (bf16[256,512]{0,1:T(8,128)(2,1)S(1)}, bf16[256,512]{0,1:T(8,128)(2,1)}, u32[]{:S(2)}) copy-start(bf16[256,512]{0,1:T(8,128)(2,1)} %copy.28) | copy-start | bytes 786436
  297.5 22.9 %copy-start.5 = (bf16[256,512]{0,1:T(8,128)(2,1)S(1)}, bf16[256,512]{0,1:T(8,128)(2,1)}, u32[]{:S(2)}) copy-start(bf16[256,512]{0,1:T(8,128)(2,1)} %get-tuple-element.15) | copy-start | bytes 786436
  302.7 8.0 %collective-permute-start.10 = (bf16[256,512]{0,1:T(8,128)(2,1)S(1)}, bf16[256,512]{0,1:T(8,128)(2,1)S(1)}, u32[]{:S(2)}, u32[]{:S(2)}) collective-permute-start(bf16[256,512]{0,1:T(8,128)(2,1)S(1)} %broadcast_select_fusion.7), channel_id=1, source_target_pairs={{8,0},{16,8},{24,16},{32,24},{40,32},{48,40},{56,48},{64,56},{72,6... | collective-permute-start | bytes 786440 | tf_op jit(solution)/shard_map/ppermute | solution.py:12
  308.4 20.1 %copy-start.14 = (f32[1,1,512]{2,1,0:T(1,128)S(1)}, f32[1,1,512]{2,1,0:T(1,128)}, u32[]{:S(2)}) copy-start(f32[1,1,512]{2,1,0:T(1,128)} %get-tuple-element.28) | copy-start | bytes 6148
  308.5 20.1 %copy-start.16 = (pred[256]{0:T(512)(128)(4,1)S(1)}, pred[256]{0:T(512)(128)(4,1)}, u32[]{:S(2)}) copy-start(pred[256]{0:T(512)(128)(4,1)} %get-tuple-element.39) | copy-start | bytes 772
  308.5 20.1 %copy-start.18 = (pred[256]{0:T(512)(128)(4,1)S(1)}, pred[256]{0:T(512)(128)(4,1)}, u32[]{:S(2)}) copy-start(pred[256]{0:T(512)(128)(4,1)} %get-tuple-element.40) | copy-start | bytes 772
  310.7 8.1 %collective-permute-start.11 = (bf16[256,512]{0,1:T(8,128)(2,1)S(1)}, bf16[256,512]{0,1:T(8,128)(2,1)S(1)}, u32[]{:S(2)}, u32[]{:S(2)}) collective-permute-start(bf16[256,512]{0,1:T(8,128)(2,1)S(1)} %broadcast_select_fusion.6), channel_id=1, source_target_pairs={{8,0},{16,8},{24,16},{32,24},{40,32},{48,40},{56,48},{64,56},{72,6... | collective-permute-start | bytes 786440 | tf_op jit(solution)/shard_map/ppermute | solution.py:12
  322.2 6.3 %collective-permute-start.13 = (bf16[2,512]{0,1:T(8,128)(2,1)S(1)}, bf16[2,512]{0,1:T(8,128)(2,1)S(1)}, u32[]{:S(2)}, u32[]{:S(2)}) collective-permute-start(bf16[2,512]{0,1:T(8,128)(2,1)S(1)} %slice.292), channel_id=1, source_target_pairs={{8,0},{16,8},{24,16},{32,24},{40,32},{48,40},{56,48},{64,56},{72,6... | collective-permute-start | bytes 6152 | tf_op jit(solution)/shard_map/ppermute | solution.py:12
  329.5 6.3 %collective-permute-start.12 = (bf16[2,512]{0,1:T(8,128)(2,1)S(1)}, bf16[2,512]{0,1:T(8,128)(2,1)S(1)}, u32[]{:S(2)}, u32[]{:S(2)}) collective-permute-start(bf16[2,512]{0,1:T(8,128)(2,1)S(1)} %slice.289), channel_id=1, source_target_pairs={{8,0},{16,8},{24,16},{32,24},{40,32},{48,40},{56,48},{64,56},{72,6... | collective-permute-start | bytes 6152 | tf_op jit(solution)/shard_map/ppermute | solution.py:12
  (15 other events, 199.5 us)
Sparse Core Ops, SparseCore 0:
  10.1 123.4 all-gather.4
  139.3 136.7 reduce-scatter.1
  288.6 79.9 all-gather.2
where the time goes:
time: 381 us; the launch traced here: 380 us
  waiting for transfers between devices  230 us (60%)
  starting transfers between devices  41.9 us (11%)
  local copies, waits for them, and re-layouts  38.2 us (10%)
  other arithmetic  28.2 us (7%)
  matrix products  23.8 us (6%)
  between operations  17.9 us (5%)
    all_gather x1, waiting for transfers between devices, local(): weight_rows = lax.all_gather(out_weight, 'ctx', axis=0, tiled=True)  126 us
    reduce_scatter x1, waiting for transfers between devices, local(): lax.psum_scatter(lax.dot_general(matched, out_grad, (((1,), (1,)), ((), (...  59.5 us
    ppermute x14, starting transfers between devices, shifted(): return lax.ppermute(array, axis, pairs)  41.8 us
    all_gather x1, waiting for transfers between devices, local(): lax.all_gather(pre_gate, 'ch', axis=1, tiled=True)  31.4 us
    reshape x4, local copies, waits for them, and re-layouts, toeplitz_tiles(): repeated.reshape(group_count, row_count, 2 * row_count - 1)  13.2 us
    unnamed x58, local copies, waits for them, and re-layouts  13.2 us
    ppermute x14, waiting for transfers between devices, shifted(): return lax.ppermute(array, axis, pairs)  12.5 us
    dot_general x4, matrix products, apply_forward(): jnp.einsum('gst,sgc->tgc', band_tile, grouped, preferred_element_type=jnp...  8.18 us
  transfers between devices with their start and end apart: 17, of which 10 were waited for; matrix products, arithmetic and copies ran while one was open for 20% of the time, Pallas kernels for 0%

commit v1 on v0

--- a/solution.py
+++ b/solution.py
@@ -142,7 +142,9 @@
     weight_rows = lax.all_gather(out_weight, "ctx", axis=0, tiled=True)
     matched = weight_rows
     out_sum = jnp.dot(
-        lax.all_gather(pre_gate, "ch", axis=1, tiled=True),
+        jnp.concatenate(
+            lax.all_to_all(jnp.stack([pre_gate] * lax.axis_size("ch")), "ch", 0, 0), axis=1
+        ),
         matched,
         preferred_element_type=jnp.float32,
     )

time: 381 us -> 370 us (0.971)
  the two profiles are of different devices: /device:TPU:8 before, /device:TPU:121 now
where the time goes in v1:
time: 370 us; the launch traced here: 368 us
  waiting for transfers between devices  215 us (58%)
  starting transfers between devices  44.5 us (12%)
  local copies, waits for them, and re-layouts  39.9 us (11%)
  other arithmetic  26.5 us (7%)
  matrix products  23.8 us (6%)
  between operations  18.3 us (5%)
    all_gather x1, waiting for transfers between devices, local(): weight_rows = lax.all_gather(out_weight, 'ctx', axis=0, tiled=True)  124 us
    reduce_scatter x1, waiting for transfers between devices, local(): lax.psum_scatter(lax.dot_general(matched, out_grad, (((1,), (1,)), ((), (...  54.4 us
    ppermute x14, starting transfers between devices, shifted(): return lax.ppermute(array, axis, pairs)  40 us
    ppermute x14, waiting for transfers between devices, shifted(): return lax.ppermute(array, axis, pairs)  35.8 us
    reshape x4, local copies, waits for them, and re-layouts, toeplitz_tiles(): repeated.reshape(group_count, row_count, 2 * row_count - 1)  13.2 us
    unnamed x58, local copies, waits for them, and re-layouts  13.2 us
    dot_general x4, matrix products, apply_forward(): jnp.einsum('gst,sgc->tgc', band_tile, grouped, preferred_element_type=jnp...  8.21 us
  transfers between devices with their start and end apart: 17, of which 10 were waited for; matrix products, arithmetic and copies ran while one was open for 20% of the time, Pallas kernels for 0%

profile of v1, /device:TPU:121, one launch (start us, length us, event | category | flops | bytes accessed | tf_op | source)
XLA Modules:
  0.0 368.2 jit_solution(11702797434304522599)
XLA Ops:
  8.0 123.5 %all-gather.2.cloned.1.call-done = bf16[4096,512]{1,0:T(8,128)(2,1)} async-done(((bf16[64,512]{1,0:T(8,128)(2,1)}), bf16[4096,512]{1,0:T(8,128)(2,1)}) %all-gather.2.cloned.1.call-update) | async-done | bytes 4194320 | tf_op jit(solution)/shard_map/all_gather | solution.py:142
  131.5 5.5 %fusion.39 = f32[4096,256]{1,0:T(8,128)} fusion(bf16[4096,512]{1,0:T(8,128)(2,1)} %all-gather.2.cloned.1.call-done, bf16[256,512]{1,0:T(8,128)(2,1)S(1)} %copy-done), kind=kOutput, calls=%fused_computation.116 | convolution fusion | flops 1073741824 | bytes 8650752 | tf_op jit(solution)/shard_map/dot_general | solution.py:153
  140.5 5.5 %collective-permute-start = (s32[2]{0:T(128)}, s32[2]{0:T(128)}, u32[]{:S(2)}, u32[]{:S(2)}) collective-permute-start(s32[2]{0:T(128)} %get-tuple-element.54), channel_id=1, source_target_pairs={{0,8},{8,16},{16,24},{24,32},{32,40},{40,48},{48,56},{56,64},{64,7... | collective-permute-start | bytes 32 | tf_op jit(solution)/shard_map/ppermute | solution.py:12
  150.2 2.7 collective-permute-start.2
  164.9 3.3 select_select_fusion.1
  168.2 2.7 collective-permute-start.5
  175.1 3.1 reshape.158
  180.4 3.0 reshape.156
  185.6 3.1 reshape.154
  192.0 4.0 %reshape.151 = bf16[4,256,511]{2,1,0:T(8,128)(2,1)} reshape(bf16[4,130816]{1,0:T(4,128)(2,1)} %slice.278) | data formatting | bytes 2093056 | tf_op jit(solution)/shard_map/reshape | solution.py:38
  204.5 7.7 %collective-permute-start.7 = (bf16[256,512]{0,1:T(8,128)(2,1)S(1)}, bf16[256,512]{0,1:T(8,128)(2,1)S(1)}, u32[]{:S(2)}, u32[]{:S(2)}) collective-permute-start(bf16[256,512]{0,1:T(8,128)(2,1)S(1)} %broadcast_select_fusion.8), channel_id=1, source_target_pairs={{0,8},{8,16},{16,24},{24,32},{32,40},{40,48},{48,56},{56,64},{64,7... | collective-permute-start | bytes 786440 | tf_op jit(solution)/shard_map/ppermute | solution.py:12
  218.0 54.4 %reduce-scatter.2.cloned.1.call-done = f32[512,256]{1,0:T(8,128)} async-done(((f32[4096,256]{1,0:T(8,128)}), f32[512,256]{1,0:T(8,128)}) %reduce-scatter.2.cloned.1.call-update) | async-done | bytes 524304 | tf_op jit(solution)/shard_map/reduce_scatter | solution.py:152
  272.5 2.8 fusion.6
  276.6 3.9 %collective-permute-start.8 = (bf16[2,512]{0,1:T(8,128)(2,1)}, bf16[2,512]{0,1:T(8,128)(2,1)}, u32[]{:S(2)}, u32[]{:S(2)}) collective-permute-start(bf16[2,512]{0,1:T(8,128)(2,1)} %slice.286), channel_id=1, source_target_pairs={{8,0},{16,8},{24,16},{32,24},{40,32},{48,40},{56,48},{64,56},{72,6... | collective-permute-start | bytes 6152 | tf_op jit(solution)/shard_map/ppermute | solution.py:12
  282.4 3.0 collective-permute-done.8
  285.3 3.5 add_convert_fusion.2
  290.3 4.4 %all-to-all-start = ((bf16[8,256,512]{1,2,0:T(8,128)(2,1)}), bf16[8,256,512]{1,2,0:T(8,128)(2,1)}, u32[]{:S(2)}, u32[]{:S(2)}) async-start(bf16[8,256,512]{1,2,0:T(8,128)(2,1)} %stack.2), calls=%async_computation | async-start | bytes 4194304 | tf_op jit(solution)/shard_map/all_to_all | solution.py:146
  297.2 2.8 select_select_fusion
  303.5 7.2 %collective-permute-done.9 = bf16[256,512]{0,1:T(8,128)(2,1)} collective-permute-done((bf16[256,512]{0,1:T(8,128)(2,1)}, bf16[256,512]{0,1:T(8,128)(2,1)}, u32[]{:S(2)}, u32[]{:S(2)}) %collective-permute-start.9) | collective-permute-done | bytes 262176 | tf_op jit(solution)/shard_map/ppermute | solution.py:12
  316.2 4.7 %collective-permute-done.10 = bf16[256,512]{0,1:T(8,128)(2,1)S(1)} collective-permute-done((bf16[256,512]{0,1:T(8,128)(2,1)S(1)}, bf16[256,512]{0,1:T(8,128)(2,1)S(1)}, u32[]{:S(2)}, u32[]{:S(2)}) %collective-permute-start.10) | collective-permute-done | bytes 262176 | tf_op jit(solution)/shard_map/ppermute | solution.py:12
  324.6 6.7 %collective-permute-done.11 = bf16[256,512]{0,1:T(8,128)(2,1)S(1)} collective-permute-done((bf16[256,512]{0,1:T(8,128)(2,1)S(1)}, bf16[256,512]{0,1:T(8,128)(2,1)S(1)}, u32[]{:S(2)}, u32[]{:S(2)}) %collective-permute-start.11) | collective-permute-done | bytes 262176 | tf_op jit(solution)/shard_map/ppermute | solution.py:12
  336.7 7.4 %collective-permute-done.13 = bf16[2,512]{0,1:T(8,128)(2,1)S(1)} collective-permute-done((bf16[2,512]{0,1:T(8,128)(2,1)S(1)}, bf16[2,512]{0,1:T(8,128)(2,1)S(1)}, u32[]{:S(2)}, u32[]{:S(2)}) %collective-permute-start.13) | collective-permute-done | bytes 2080 | tf_op jit(solution)/shard_map/ppermute | solution.py:12
  348.7 5.8 %collective-permute-done.12 = bf16[2,512]{0,1:T(8,128)(2,1)S(1)} collective-permute-done((bf16[2,512]{0,1:T(8,128)(2,1)S(1)}, bf16[2,512]{0,1:T(8,128)(2,1)S(1)}, u32[]{:S(2)}, u32[]{:S(2)}) %collective-permute-start.12) | collective-permute-done | bytes 2080 | tf_op jit(solution)/shard_map/ppermute | solution.py:12
  356.6 4.8 %convolution_convert_fusion = bf16[256,512]{1,0:T(8,128)(2,1)} fusion(bf16[256,4096]{0,1:T(8,128)(2,1)} %bitcast.25, bf16[4096,512]{1,0:T(8,128)(2,1)} %all-gather.2.cloned.1.call-done), kind=kOutput, calls=%fused_computation | convolution fusion | flops 1073872896 | bytes 6553600 | tf_op jit(solution)/shard_map/dot_general | solution.py:144
  (132 shorter events, 74.4 us)
Async XLA Ops:
  7.2 124.3 %copy-start = (bf16[256,512]{1,0:T(8,128)(2,1)S(1)}, bf16[256,512]{1,0:T(8,128)(2,1)}, u32[]{:S(2)}) copy-start(bf16[256,512]{1,0:T(8,128)(2,1)} %param.17) | copy-start | bytes 786436
  7.2 124.3 %all-gather.2.cloned.1.call-start = ((), (), s32[]{:S(2)}) async-start(), calls=%async_computation.2 | async-start | bytes 4259840 | tf_op jit(solution)/shard_map/all_gather | solution.py:142
  7.9 264.6 %reduce-scatter.2.cloned.1.call-start = ((), (), s32[]{:S(2)}) async-start(), calls=%async_computation.3 | async-start | bytes 4718592 | tf_op jit(solution)/shard_map/reduce_scatter | solution.py:152
  138.3 22.0 %collective-permute-start.4 = (s32[2]{0:T(128)}, s32[2]{0:T(128)}, u32[]{:S(2)}, u32[]{:S(2)}) collective-permute-start(s32[2]{0:T(128)} %get-tuple-element.55), channel_id=1, source_target_pairs={{8,0},{16,8},{24,16},{32,24},{40,32},{48,40},{56,48},{64,56},{72,6... | collective-permute-start | bytes 32 | tf_op jit(solution)/shard_map/ppermute | solution.py:12
  140.5 20.5 %collective-permute-start = (s32[2]{0:T(128)}, s32[2]{0:T(128)}, u32[]{:S(2)}, u32[]{:S(2)}) collective-permute-start(s32[2]{0:T(128)} %get-tuple-element.54), channel_id=1, source_target_pairs={{0,8},{8,16},{16,24},{24,32},{32,40},{40,48},{48,56},{56,64},{64,7... | collective-permute-start | bytes 32 | tf_op jit(solution)/shard_map/ppermute | solution.py:12
  147.5 134.9 %collective-permute-start.1 = (bf16[2,512]{0,1:T(8,128)(2,1)}, bf16[2,512]{0,1:T(8,128)(2,1)}, u32[]{:S(2)}, u32[]{:S(2)}) collective-permute-start(bf16[2,512]{0,1:T(8,128)(2,1)} %copy.27), channel_id=1, source_target_pairs={{0,8},{8,16},{16,24},{24,32},{32,40},{40,48},{48,56},{56,64},{64,7... | collective-permute-start | bytes 6152 | tf_op jit(solution)/shard_map/ppermute | solution.py:12
  150.2 14.6 %collective-permute-start.2 = (bf16[2,512]{0,1:T(8,128)(2,1)}, bf16[2,512]{0,1:T(8,128)(2,1)}, u32[]{:S(2)}, u32[]{:S(2)}) collective-permute-start(bf16[2,512]{0,1:T(8,128)(2,1)} %copy.30), channel_id=1, source_target_pairs={{0,8},{8,16},{16,24},{24,32},{32,40},{40,48},{48,56},{56,64},{64,7... | collective-permute-start | bytes 6152 | tf_op jit(solution)/shard_map/ppermute | solution.py:12
  153.8 11.1 %collective-permute-start.3 = (bf16[2,512]{0,1:T(8,128)(2,1)}, bf16[2,512]{0,1:T(8,128)(2,1)S(1)}, u32[]{:S(2)}, u32[]{:S(2)}) collective-permute-start(bf16[2,512]{0,1:T(8,128)(2,1)} %copy.33), channel_id=1, source_target_pairs={{0,8},{8,16},{16,24},{24,32},{32,40},{40,48},{48,56},{56,64},{64,7... | collective-permute-start | bytes 6152 | tf_op jit(solution)/shard_map/ppermute | solution.py:12
  168.2 30.0 %collective-permute-start.5 = (bf16[256,512]{0,1:T(8,128)(2,1)}, bf16[256,512]{0,1:T(8,128)(2,1)}, u32[]{:S(2)}, u32[]{:S(2)}) collective-permute-start(bf16[256,512]{0,1:T(8,128)(2,1)} %get-tuple-element.18), channel_id=1, source_target_pairs={{0,8},{8,16},{16,24},{24,32},{32,40},{40,48},{48,56},{56,64},{64,7... | collective-permute-start | bytes 786440 | tf_op jit(solution)/shard_map/ppermute | solution.py:12
  198.3 6.2 %collective-permute-start.6 = (bf16[256,512]{0,1:T(8,128)(2,1)S(1)}, bf16[256,512]{0,1:T(8,128)(2,1)S(1)}, u32[]{:S(2)}, u32[]{:S(2)}) collective-permute-start(bf16[256,512]{0,1:T(8,128)(2,1)S(1)} %broadcast_select_fusion.9), channel_id=1, source_target_pairs={{0,8},{8,16},{16,24},{24,32},{32,40},{40,48},{48,56},{56,64},{64,7... | collective-permute-start | bytes 786440 | tf_op jit(solution)/shard_map/ppermute | solution.py:12
  204.5 80.9 %copy-start.10 = (pred[256]{0:T(512)(128)(4,1)S(1)}, pred[256]{0:T(512)(128)(4,1)}, u32[]{:S(2)}) copy-start(pred[256]{0:T(512)(128)(4,1)} %get-tuple-element.45) | copy-start | bytes 772
  204.5 11.1 %collective-permute-start.7 = (bf16[256,512]{0,1:T(8,128)(2,1)S(1)}, bf16[256,512]{0,1:T(8,128)(2,1)S(1)}, u32[]{:S(2)}, u32[]{:S(2)}) collective-permute-start(bf16[256,512]{0,1:T(8,128)(2,1)S(1)} %broadcast_select_fusion.8), channel_id=1, source_target_pairs={{0,8},{8,16},{16,24},{24,32},{32,40},{40,48},{48,56},{56,64},{64,7... | collective-permute-start | bytes 786440 | tf_op jit(solution)/shard_map/ppermute | solution.py:12
  276.6 8.7 %collective-permute-start.8 = (bf16[2,512]{0,1:T(8,128)(2,1)}, bf16[2,512]{0,1:T(8,128)(2,1)}, u32[]{:S(2)}, u32[]{:S(2)}) collective-permute-start(bf16[2,512]{0,1:T(8,128)(2,1)} %slice.286), channel_id=1, source_target_pairs={{8,0},{16,8},{24,16},{32,24},{40,32},{48,40},{56,48},{64,56},{72,6... | collective-permute-start | bytes 6152 | tf_op jit(solution)/shard_map/ppermute | solution.py:12
  290.3 66.3 %all-to-all-start = ((bf16[8,256,512]{1,2,0:T(8,128)(2,1)}), bf16[8,256,512]{1,2,0:T(8,128)(2,1)}, u32[]{:S(2)}, u32[]{:S(2)}) async-start(bf16[8,256,512]{1,2,0:T(8,128)(2,1)} %stack.2), calls=%async_computation | async-start | bytes 4194304 | tf_op jit(solution)/shard_map/all_to_all | solution.py:146
  300.0 10.6 %collective-permute-start.9 = (bf16[256,512]{0,1:T(8,128)(2,1)}, bf16[256,512]{0,1:T(8,128)(2,1)}, u32[]{:S(2)}, u32[]{:S(2)}) collective-permute-start(bf16[256,512]{0,1:T(8,128)(2,1)} %get-tuple-element.14), channel_id=1, source_target_pairs={{8,0},{16,8},{24,16},{32,24},{40,32},{48,40},{56,48},{64,56},{72,6... | collective-permute-start | bytes 786440 | tf_op jit(solution)/shard_map/ppermute | solution.py:12
  302.0 31.0 %copy-start.2 = (bf16[256,512]{0,1:T(8,128)(2,1)S(1)}, bf16[256,512]{0,1:T(8,128)(2,1)}, u32[]{:S(2)}) copy-start(bf16[256,512]{0,1:T(8,128)(2,1)} %copy.29) | copy-start | bytes 786436
  302.0 31.0 %copy-start.5 = (bf16[256,512]{0,1:T(8,128)(2,1)S(1)}, bf16[256,512]{0,1:T(8,128)(2,1)}, u32[]{:S(2)}) copy-start(bf16[256,512]{0,1:T(8,128)(2,1)} %get-tuple-element.15) | copy-start | bytes 786436
  310.7 10.3 %collective-permute-start.10 = (bf16[256,512]{0,1:T(8,128)(2,1)S(1)}, bf16[256,512]{0,1:T(8,128)(2,1)S(1)}, u32[]{:S(2)}, u32[]{:S(2)}) collective-permute-start(bf16[256,512]{0,1:T(8,128)(2,1)S(1)} %broadcast_select_fusion.7), channel_id=1, source_target_pairs={{8,0},{16,8},{24,16},{32,24},{40,32},{48,40},{56,48},{64,56},{72,6... | collective-permute-start | bytes 786440 | tf_op jit(solution)/shard_map/ppermute | solution.py:12
  314.3 29.9 %copy-start.14 = (f32[1,1,512]{2,1,0:T(1,128)S(1)}, f32[1,1,512]{2,1,0:T(1,128)}, u32[]{:S(2)}) copy-start(f32[1,1,512]{2,1,0:T(1,128)} %get-tuple-element.28) | copy-start | bytes 6148
  314.3 29.9 %copy-start.16 = (pred[256]{0:T(512)(128)(4,1)S(1)}, pred[256]{0:T(512)(128)(4,1)}, u32[]{:S(2)}) copy-start(pred[256]{0:T(512)(128)(4,1)} %get-tuple-element.39) | copy-start | bytes 772
  314.3 29.9 %copy-start.18 = (pred[256]{0:T(512)(128)(4,1)S(1)}, pred[256]{0:T(512)(128)(4,1)}, u32[]{:S(2)}) copy-start(pred[256]{0:T(512)(128)(4,1)} %get-tuple-element.40) | copy-start | bytes 772
  321.0 10.3 %collective-permute-start.11 = (bf16[256,512]{0,1:T(8,128)(2,1)S(1)}, bf16[256,512]{0,1:T(8,128)(2,1)S(1)}, u32[]{:S(2)}, u32[]{:S(2)}) collective-permute-start(bf16[256,512]{0,1:T(8,128)(2,1)S(1)} %broadcast_select_fusion.6), channel_id=1, source_target_pairs={{8,0},{16,8},{24,16},{32,24},{40,32},{48,40},{56,48},{64,56},{72,6... | collective-permute-start | bytes 786440 | tf_op jit(solution)/shard_map/ppermute | solution.py:12
  334.8 9.3 %collective-permute-start.13 = (bf16[2,512]{0,1:T(8,128)(2,1)S(1)}, bf16[2,512]{0,1:T(8,128)(2,1)S(1)}, u32[]{:S(2)}, u32[]{:S(2)}) collective-permute-start(bf16[2,512]{0,1:T(8,128)(2,1)S(1)} %slice.292), channel_id=1, source_target_pairs={{8,0},{16,8},{24,16},{32,24},{40,32},{48,40},{56,48},{64,56},{72,6... | collective-permute-start | bytes 6152 | tf_op jit(solution)/shard_map/ppermute | solution.py:12
  345.0 9.4 %collective-permute-start.12 = (bf16[2,512]{0,1:T(8,128)(2,1)S(1)}, bf16[2,512]{0,1:T(8,128)(2,1)S(1)}, u32[]{:S(2)}, u32[]{:S(2)}) collective-permute-start(bf16[2,512]{0,1:T(8,128)(2,1)S(1)} %slice.289), channel_id=1, source_target_pairs={{8,0},{16,8},{24,16},{32,24},{40,32},{48,40},{56,48},{64,56},{72,6... | collective-permute-start | bytes 6152 | tf_op jit(solution)/shard_map/ppermute | solution.py:12
  (15 other events, 264.6 us)
Sparse Core Ops, SparseCore 0:
  10.1 121.3 all-gather.1
  137.2 135.2 reduce-scatter.1
